TPU v7x, 32 devices: a whole 2x2x4 slice. The times are simulated.
32 devices in a mesh: expert: 4 (over y, x), dp: 8 (over z, core).
Axes of the slice: x: 2, y: 2, z: 4, core: 2. Of those that a mesh axis runs over, the one named last changes fastest.
Arguments:
- routes: int32 [4096, 2], P(('expert', 'dp')), may hold values from 0 to 1, as said below
- expert_inputs: bfloat16 [8, 4, 512, 2048], P('dp', 'expert'), may hold values from -6 to 6
- hidden_grad: bfloat16 [8, 4, 512, 2048], P('dp', 'expert'), may hold values from -6 to 6
- weight: float32 [2048, 8192], P('dp', 'expert'), may hold values from -0.125 to 0.125
- moment_one: float32 [2048, 8192], P('dp', 'expert'), may hold values from -6 to 6
- moment_two: float32 [2048, 8192], P('dp', 'expert'), may hold values from 0.5 to 4
Outputs:
- token_grad: bfloat16 [4096, 2048], P(('expert', 'dp'))
- new_weight: float32 [2048, 8192], P('dp', 'expert')
- new_first: float32 [2048, 8192], P('dp', 'expert')
- new_second: float32 [2048, 8192], P('dp', 'expert')
Inputs may be any that keep to these rules, and one draw needn't show every extreme that they name: `routes`: each token names 2 different experts; the tokens of one device name one expert at most 128 times, and in every device's tokens some expert is named exactly 128 times.
All inputs are finite; a program needn't handle non-finite values.
Results may differ from a plain program's by a relative error of at most 0.0045.
The roundings to bfloat16 on the way count: a program that leaves them out, or rounds other values in their place, can miss the bound.
Values may be sent and summed in bfloat16 or wider, within the bound.
No kernel may reach another device: no remote copies, remote signals or barrier semaphores. Data moves between devices by JAX's collectives and lax.ppermute only.
A program may use at most 128 MiB of HBM per device.

v0:
```python
import jax
import jax.numpy as jnp
from jax import lax
from jax.sharding import PartitionSpec as P

beta_one = 0.9
beta_two = 0.95
learn_rate = 0.003
decay = 0.1
epsilon = 1e-08
loss_scale = 64.0
bias_one = 1.0 - (0.9**50) ** 2
bias_two = 1.0 - (0.95**50) ** 2


def adamw(weight, moment_one, moment_two, grad):
    new_first = beta_one * moment_one + (1.0 - beta_one) * grad
    new_second = beta_two * moment_two + (1.0 - beta_two) * grad * grad
    update = new_first / bias_one / (jnp.sqrt(new_second / bias_two) + epsilon)
    new_weight = weight - learn_rate * (update + decay * weight)
    return (new_weight, new_first, new_second)


def shards(routes, expert_inputs, hidden_grad, weight, moment_one, moment_two):
    n_expert = lax.axis_size("expert")
    experts = n_expert // 2
    slot_rows = expert_inputs.shape[2]
    capacity = slot_rows // n_expert
    width = expert_inputs.shape[3]
    tok_count = routes.shape[0]
    top_count = routes.shape[1]
    flat_routes = routes.reshape(-1)
    onehot = (flat_routes[:, None] == jnp.arange(experts, dtype=jnp.int32)[None, :]).astype(
        jnp.int32
    )
    running = jnp.cumsum(onehot, axis=0)
    slots = jnp.sum((running - 1) * onehot, axis=1).reshape(tok_count, top_count)
    counts = jnp.sum(onehot, axis=0)
    all_counts = lax.all_gather(counts[None, :], "expert", axis=0, tiled=True)
    my_expert = lax.axis_index("expert") // 2
    chosen = jnp.arange(experts, dtype=jnp.int32)[None, :] == my_expert
    my_counts = jnp.sum(jnp.where(chosen, all_counts, 0), axis=1)
    valid = (jnp.arange(capacity, dtype=jnp.int32)[None, :] < my_counts[:, None]).reshape(-1)
    inputs_flat = expert_inputs.reshape(slot_rows, width)
    grad_flat = hidden_grad.reshape(slot_rows, -1)
    masked = jnp.where(valid[:, None], grad_flat, jnp.zeros_like(grad_flat))
    wbf = weight.astype(jnp.bfloat16)
    partial_rows = lax.dot_general(
        masked,
        lax.all_gather(wbf, "dp", axis=0, tiled=True),
        (((1,), (1,)), ((), ())),
        preferred_element_type=jnp.float32,
    )
    sent = partial_rows.reshape(n_expert, capacity, width)
    received = lax.all_to_all(sent, "expert", split_axis=0, concat_axis=0, tiled=True)
    paired = jnp.sum(received.reshape(experts, 2, capacity, width), axis=1).astype(jnp.bfloat16)
    picked = paired[routes, slots]
    token_grad = jnp.sum(picked.astype(jnp.float32), axis=1).astype(jnp.bfloat16)
    owned = lax.psum_scatter(
        lax.dot_general(
            inputs_flat, masked, (((0,), (0,)), ((), ())), preferred_element_type=jnp.float32
        ).astype(jnp.bfloat16),
        "dp",
        scatter_dimension=0,
        tiled=True,
    ).astype(jnp.float32)
    new_weight, new_first, new_second = adamw(weight, moment_one, moment_two, owned / loss_scale)
    return (token_grad, new_weight, new_first, new_second)


def solution(mesh):
    in_specs = (
        P(("expert", "dp"), None),
        P("dp", "expert", None, None),
        P("dp", "expert", None, None),
        P("dp", "expert"),
        P("dp", "expert"),
        P("dp", "expert"),
    )
    out_specs = (P(("expert", "dp"), None), P("dp", "expert"), P("dp", "expert"), P("dp", "expert"))
    return jax.shard_map(shards, mesh=mesh, in_specs=in_specs, out_specs=out_specs, check_vma=False)
```

profile of v0, /device:TPU:0, one launch (start us, length us, event | category | flops | bytes accessed | tf_op | source)
XLA Modules:
  0.0 221.4 jit_solution(1023216353679421165)
XLA Ops:
  7.2 2.9 %convert_element_type.25 = bf16[256,2048]{1,0:T(8,128)(2,1)} convert(f32[256,2048]{1,0:T(8,128)} %param.9) | non-fusion elementwise | flops 524288 | bytes 3145728 | tf_op jit(solution)/shard_map/convert_element_type | solution.py:47
  10.6 0.6 reduce-window.6
  11.2 0.2 slice_reduce_fusion
  11.4 0.2 reduce-window.9
  11.6 0.6 dynamic-slice
  13.1 0.2 dynamic-update-slice
  13.3 8.8 %all-reduce = s32[8]{0:T(128)S(1)} all-reduce(s32[8]{0:T(128)S(1)} %dynamic-update-slice), channel_id=2, replica_groups=mesh['expert'=4,'dp'=8] {'expert'}, use_global_device_ids=true, to_apply=%add | all-reduce | flops 8 | bytes 64
  22.4 8.8 %convert_bitcast_fusion = bf16[2048,2048]{0,1:T(8,128)(2,1)} fusion(bf16[1,1,512,2048]{3,2,1,0:T(8,128)(2,1)S(1)} %copy-done, bf16[1,1,512,2048]{3,2,1,0:T(8,128)(2,1)} %param.8, pred[512]{0:T(512)(128)(4,1)S(1)} %get-tuple-element.21), kind=kOutput, calls=%fused_computation.3 | convolution fusion | flops 4300210176 | bytes 12583424 | tf_op jit(solution)/shard_map/dot_general | solution.py:60
  31.2 63.8 %all-gather.3.cloned.1.call-done = bf16[2048,2048]{1,0:T(8,128)(2,1)} async-done(((bf16[256,2048]{1,0:T(8,128)(2,1)}), bf16[2048,2048]{1,0:T(8,128)(2,1)}) %all-gather.3.cloned.1.call-update) | async-done | bytes 8388624 | tf_op jit(solution)/shard_map/all_gather | solution.py:50
  95.0 10.5 %fusion = f32[4,128,2048]{2,1,0:T(8,128)} fusion(bf16[2048,2048]{1,0:T(8,128)(2,1)} %all-gather.3.cloned.1.call-done, bf16[4,128,2048]{2,1,0:T(8,128)(2,1)} %bitcast.39, pred[4,128]{1,0:T(4,128)(4,1)S(1)} %get-tuple-element.22), kind=kOutput, calls=%fused_computation.1 | convolution fusion | flops 4296015872 | bytes 14680576 | tf_op jit(solution)/shard_map/dot_general | solution.py:48
  105.6 5.1 %all-to-all-start = ((f32[4,128,2048]{2,1,0:T(8,128)}), f32[4,128,2048]{2,1,0:T(8,128)}, u32[]{:S(2)}, u32[]{:S(2)}) async-start(f32[4,128,2048]{2,1,0:T(8,128)} %fusion), calls=%async_computation | async-start | bytes 8388608 | tf_op jit(solution)/shard_map/all_to_all | solution.py:55
  110.7 2.9 %copy.40 = f32[256,2048]{0,1:T(8,128)} copy(f32[256,2048]{1,0:T(8,128)} %param.9) | data formatting | bytes 4194304 | tf_op args[3]
  113.9 0.1 reshape.108
  114.1 2.9 %copy.37 = f32[256,2048]{0,1:T(8,128)} copy(f32[256,2048]{1,0:T(8,128)} %param.10) | data formatting | bytes 4194304 | tf_op args[4]
  117.0 2.9 %copy.38 = f32[256,2048]{0,1:T(8,128)} copy(f32[256,2048]{1,0:T(8,128)} %param.11) | data formatting | bytes 4194304 | tf_op args[5]
  119.9 65.6 %reduce-scatter.2.cloned.1.call-done = bf16[256,2048]{0,1:T(8,128)(2,1)} async-done(((bf16[2048,2048]{0,1:T(8,128)(2,1)}), bf16[256,2048]{0,1:T(8,128)(2,1)}) %reduce-scatter.2.cloned.1.call-update) | async-done | bytes 1048592 | tf_op jit(solution)/shard_map/reduce_scatter | solution.py:59
  185.5 7.0 %multiply_subtract_fusion = (f32[256,2048]{0,1:T(8,128)}, f32[256,2048]{0,1:T(8,128)}, f32[256,2048]{0,1:T(8,128)}) fusion(f32[256,2048]{0,1:T(8,128)} %copy.40, bf16[256,2048]{0,1:T(8,128)(2,1)} %reduce-scatter.2.cloned.1.call-done, f32[256,2048]{0,1:T(8,128)} %copy.37, f32[256,2048]{0,1:T(8,128)} %copy.38), kind=kLoop, calls=%fused_computation.13 | loop fusion | flops 8912896 | bytes 13631488 | tf_op jit(solution)/shard_map/sub | solution.py:20
  192.5 2.9 %copy.41 = f32[256,2048]{1,0:T(8,128)} copy(f32[256,2048]{0,1:T(8,128)} %get-tuple-element.18) | data formatting | bytes 4194304
  195.4 2.9 %copy.42 = f32[256,2048]{1,0:T(8,128)} copy(f32[256,2048]{0,1:T(8,128)} %get-tuple-element.19) | data formatting | bytes 4194304
  198.2 2.9 %copy.43 = f32[256,2048]{1,0:T(8,128)} copy(f32[256,2048]{0,1:T(8,128)} %get-tuple-element.20) | data formatting | bytes 4194304
  201.1 2.7 %bitcast_reduce_fusion = bf16[2,128,2048]{2,1,0:T(8,128)(2,1)S(1)} fusion(f32[4,128,2048]{2,1,0:T(8,128)} %all-to-all-done), kind=kLoop, calls=%fused_computation.4 | loop fusion | flops 524288 | bytes 5242880 | tf_op jit(solution)/shard_map/reduce_sum | solution.py:56
  203.9 5.3 %gather_fusion = bf16[256,2048]{1,0:T(8,128)(2,1)} fusion(bf16[2,128,2048]{2,1,0:T(8,128)(2,1)S(1)} %bitcast_reduce_fusion, s32[256]{0:T(256)S(1)} %reshape.108), kind=kCustom, calls=%fused_computation | custom fusion | bytes 2099200 | tf_op jit(solution)/shard_map/gather | solution.py:57
  209.2 1.7 reshape.111
  210.9 3.6 %reduce_sum.52 = bf16[128,2048]{1,0:T(8,128)(2,1)} reduce(bf16[128,2,2048]{2,1,0:T(2,128)(2,1)S(1)} %reshape.111, bf16[]{:T(256)} %constant.46.clone.1), dimensions={1}, to_apply=%region_6.7 | reduce | flops 262144 | bytes 1572866 | tf_op jit(solution)/shard_map/reduce_sum | solution.py:58
  (26 shorter events, 1.3 us)
Async XLA Ops:
  7.2 15.2 %copy-start = (bf16[1,1,512,2048]{3,2,1,0:T(8,128)(2,1)S(1)}, bf16[1,1,512,2048]{3,2,1,0:T(8,128)(2,1)}, u32[]{:S(2)}) copy-start(bf16[1,1,512,2048]{3,2,1,0:T(8,128)(2,1)} %param.7) | copy-start | bytes 6291460
  7.2 4.4 %copy-start.2 = (u32[32]{0:T(128)S(1)}, u32[32]{0:T(128)}, u32[]{:S(2)}) copy-start(u32[32]{0:T(128)} %constant.77) | copy-start | bytes 388
  7.2 3.0 %copy-start.1 = (s32[128,2]{0,1:T(2,128)S(1)}, s32[128,2]{0,1:T(2,128)}, u32[]{:S(2)}) copy-start(s32[128,2]{0,1:T(2,128)} %param.6) | copy-start | bytes 3076
  7.2 87.8 %all-gather.3.cloned.1.call-start = ((), (), s32[]{:S(2)}) async-start(), calls=%async_computation.2 | async-start | bytes 9437184 | tf_op jit(solution)/shard_map/all_gather | solution.py:50
  10.1 175.4 %reduce-scatter.2.cloned.1.call-start = ((), (), s32[]{:S(2)}) async-start(), calls=%async_computation.3 | async-start | bytes 9437184 | tf_op jit(solution)/shard_map/reduce_scatter | solution.py:59
  105.6 95.5 %all-to-all-start = ((f32[4,128,2048]{2,1,0:T(8,128)}), f32[4,128,2048]{2,1,0:T(8,128)}, u32[]{:S(2)}, u32[]{:S(2)}) async-start(f32[4,128,2048]{2,1,0:T(8,128)} %fusion), calls=%async_computation | async-start | bytes 8388608 | tf_op jit(solution)/shard_map/all_to_all | solution.py:55
Sparse Core Ops, SparseCore 0:
  10.2 84.7 all-gather.2
  97.3 88.1 reduce-scatter.1
where the time goes:
time: 222 us; the launch traced here: 221 us
  waiting for transfers between devices  129 us (58%)
  local copies, waits for them, and re-layouts  26.4 us (12%)
  matrix products  19.4 us (9%)
  other arithmetic  17.4 us (8%)
  between operations  14.8 us (7%)
  blocking collectives  8.82 us (4%)
  starting transfers between devices  5.2 us (2%)
    reduce_scatter x1, waiting for transfers between devices, shards(): lax.psum_scatter(lax.dot_general(inputs_flat, masked, (((0,), (0,)), ((),...  65.6 us
    all_gather x1, waiting for transfers between devices, shards(): lax.all_gather(wbf, 'dp', axis=0, tiled=True)  63.8 us
    unnamed x16, local copies, waits for them, and re-layouts  18.3 us
    dot_general x1, matrix products, shards(): lax.dot_general(masked, lax.all_gather(wbf, 'dp', axis=0, tiled=True), ((...  10.5 us
    unnamed x1, blocking collectives  8.82 us
    dot_general x1, matrix products, shards(): lax.dot_general(inputs_flat, masked, (((0,), (0,)), ((), ())), preferred_...  8.81 us
    gather x2, local copies, waits for them, and re-layouts, shards(): picked = paired[routes, slots]  7.06 us
    sub x1, other arithmetic, adamw(): new_weight = weight - learn_rate * (update + decay * weight)  6.97 us
  transfers between devices with their start and end apart: 3, of which 2 were waited for; matrix products, arithmetic and copies ran while one was open for 21% of the time, Pallas kernels for 0%

commit v1 on v0

--- a/solution.py
+++ b/solution.py
@@ -11,6 +11,28 @@
 loss_scale = 64.0
 bias_one = 1.0 - (0.9**50) ** 2
 bias_two = 1.0 - (0.95**50) ** 2
+
+
+def in_order(pieces, dim):
+    lengths = list(pieces.shape[1:])
+    lengths[dim] *= pieces.shape[0]
+    return jnp.moveaxis(pieces, 0, dim).reshape(lengths)
+
+
+def collect(value, axis, dim):
+    peers = lax.axis_size(axis)
+    pairs = [(i, (i + 1) % peers) for i in range(peers)]
+    back = [(b, a) for a, b in pairs]
+    lower, upper = ([], [])
+    for turn in range(peers - 1):
+        if turn % 2 == 0:
+            lower.append(lax.ppermute(lower[-1] if lower else value, axis, pairs))
+        else:
+            upper.append(lax.ppermute(upper[-1] if upper else value, axis, back))
+    blocks = jnp.stack([*lower[::-1], value, *upper])
+    shift = lax.axis_index(axis) - len(lower)
+    blocks = blocks[(jnp.arange(peers) - shift) % peers]
+    return in_order(blocks, dim)
 
 
 def adamw(weight, moment_one, moment_two, grad):
@@ -46,10 +68,7 @@
     masked = jnp.where(valid[:, None], grad_flat, jnp.zeros_like(grad_flat))
     wbf = weight.astype(jnp.bfloat16)
     partial_rows = lax.dot_general(
-        masked,
-        lax.all_gather(wbf, "dp", axis=0, tiled=True),
-        (((1,), (1,)), ((), ())),
-        preferred_element_type=jnp.float32,
+        masked, collect(wbf, "dp", 0), (((1,), (1,)), ((), ())), preferred_element_type=jnp.float32
     )
     sent = partial_rows.reshape(n_expert, capacity, width)
     received = lax.all_to_all(sent, "expert", split_axis=0, concat_axis=0, tiled=True)

time: 222 us -> 310 us (1.40)
  waiting for transfers between devices: 129 us -> 186 us
  local copies, waits for them, and re-layouts: 26.4 us -> 48.9 us
  starting transfers between devices: 5.2 us -> 15.6 us
    ppermute x0 -> x7, waiting for transfers between devices: none -> 151 us  [the longest x4 150 us: collect(): lower.append(lax.ppermute(lower[-1] if lower else value, axis, pairs))]
    reduce_scatter x1, waiting for transfers between devices: 65.6 us -> 0.01 us  [shards(): lax.psum_scatter(lax.dot_general(inputs_flat, masked, (((0,), (0,)), ((),...]
    all_gather x1 -> x0, waiting for transfers between devices: 63.8 us -> none  [shards(): lax.all_gather(wbf, 'dp', axis=0, tiled=True)]
    all_to_all x1, waiting for transfers between devices: 0.01 us -> 35.3 us  [shards(): lax.all_to_all(sent, 'expert', split_axis=0, concat_axis=0, tiled=True)]
    unnamed x16 -> x34, local copies, waits for them, and re-layouts: 18.3 us -> 32.8 us
    ppermute x0 -> x7, starting transfers between devices: none -> 10.5 us  [the longest x3 10.4 us: collect(): upper.append(lax.ppermute(upper[-1] if upper else value, axis, back))]
    gather x0 -> x1, local copies, waits for them, and re-layouts: none -> 8.05 us  [collect(): blocks = blocks[(jnp.arange(peers) - shift) % peers]]
  transfers between devices with their start and end apart: 3 -> 9, of which waited for: 2 -> 7; matrix products, arithmetic and copies ran while one was open for 21% -> 17% of each run, Pallas kernels for 0% -> 0%
where the time goes in v1:
time: 310 us
  waiting for transfers between devices  186 us (60%)
  local copies, waits for them, and re-layouts  48.9 us (16%)
  other arithmetic  18 us (6%)
  matrix products  17.4 us (6%)
  starting transfers between devices  15.6 us (5%)
  between operations  14.9 us (5%)
  blocking collectives  8.83 us (3%)
    ppermute x4, waiting for transfers between devices, collect(): lower.append(lax.ppermute(lower[-1] if lower else value, axis, pairs))  150 us
    all_to_all x1, waiting for transfers between devices, shards(): lax.all_to_all(sent, 'expert', split_axis=0, concat_axis=0, tiled=True)  35.3 us
    unnamed x34, local copies, waits for them, and re-layouts  32.8 us
    dot_general x1, matrix products, shards(): lax.dot_general(masked, collect(wbf, 'dp', 0), (((1,), (1,)), ((), ())),...  10.5 us
    ppermute x3, starting transfers between devices, collect(): upper.append(lax.ppermute(upper[-1] if upper else value, axis, back))  10.4 us
    unnamed x1, blocking collectives  8.83 us
    gather x1, local copies, waits for them, and re-layouts, collect(): blocks = blocks[(jnp.arange(peers) - shift) % peers]  8.05 us
    dot_general x1, matrix products, shards(): lax.dot_general(inputs_flat, masked, (((0,), (0,)), ((), ())), preferred_...  6.83 us
  transfers between devices with their start and end apart: 9, of which 7 were waited for; matrix products, arithmetic and copies ran while one was open for 17% of the time, Pallas kernels for 0%

profile of v1, /device:TPU:0, one launch (start us, length us, event | category | flops | bytes accessed | tf_op | source)
XLA Modules:
  0.0 309.8 jit_solution(15714090881878481912)
XLA Ops:
  11.8 8.8 %all-reduce = s32[8]{0:T(128)S(1)} all-reduce(s32[8]{0:T(128)S(1)} %dynamic-update-slice), channel_id=2, replica_groups=mesh['expert'=4,'dp'=8] {'expert'}, use_global_device_ids=true, to_apply=%add | all-reduce | flops 8 | bytes 64
  24.1 6.8 %convert_bitcast_fusion = bf16[2048,2048]{0,1:T(8,128)(2,1)} fusion(bf16[1,1,512,2048]{3,2,1,0:T(8,128)(2,1)S(1)} %copy-done, bf16[1,1,512,2048]{3,2,1,0:T(8,128)(2,1)S(1)} %broadcast_select_fusion), kind=kOutput, calls=%fused_computation.2 | convolution fusion | flops 4299161600 | bytes 12582912 | tf_op jit(solution)/shard_map/dot_general | solution.py:79
  32.7 30.9 %collective-permute-done = bf16[256,2048]{1,0:T(8,128)(2,1)S(1)} collective-permute-done((bf16[256,2048]{1,0:T(8,128)(2,1)S(1)}, bf16[256,2048]{1,0:T(8,128)(2,1)S(1)}, u32[]{:S(2)}, u32[]{:S(2)}) %collective-permute-start) | collective-permute-done | bytes 1048608 | tf_op jit(solution)/shard_map/ppermute | solution.py:29
  63.7 3.5 %collective-permute-start.4 = (bf16[256,2048]{1,0:T(8,128)(2,1)S(1)}, bf16[256,2048]{1,0:T(8,128)(2,1)}, u32[]{:S(2)}, u32[]{:S(2)}) collective-permute-start(bf16[256,2048]{1,0:T(8,128)(2,1)S(1)} %convert_element_type.25), channel_id=1, source_target_pairs={{1,0},{2,1},{3,2},{4,3},{5,4},{6,5},{7,6},{0,7},{9,8},{10,9},{11,1... | collective-permute-start | bytes 3145736 | tf_op jit(solution)/shard_map/ppermute | solution.py:31
  67.2 45.3 %collective-permute-done.1 = bf16[256,2048]{1,0:T(8,128)(2,1)S(1)} collective-permute-done((bf16[256,2048]{1,0:T(8,128)(2,1)S(1)}, bf16[256,2048]{1,0:T(8,128)(2,1)S(1)}, u32[]{:S(2)}, u32[]{:S(2)}) %collective-permute-start.1) | collective-permute-done | bytes 1048608 | tf_op jit(solution)/shard_map/ppermute | solution.py:29
  113.5 3.2 %collective-permute-start.5 = (bf16[256,2048]{1,0:T(8,128)(2,1)}, bf16[256,2048]{1,0:T(8,128)(2,1)}, u32[]{:S(2)}, u32[]{:S(2)}) collective-permute-start(bf16[256,2048]{1,0:T(8,128)(2,1)} %collective-permute-done.4), channel_id=1, source_target_pairs={{1,0},{2,1},{3,2},{4,3},{5,4},{6,5},{7,6},{0,7},{9,8},{10,9},{11,1... | collective-permute-start | bytes 3145736 | tf_op jit(solution)/shard_map/ppermute | solution.py:31
  116.6 45.1 %collective-permute-done.2 = bf16[256,2048]{1,0:T(8,128)(2,1)} collective-permute-done((bf16[256,2048]{1,0:T(8,128)(2,1)S(1)}, bf16[256,2048]{1,0:T(8,128)(2,1)}, u32[]{:S(2)}, u32[]{:S(2)}) %collective-permute-start.2) | collective-permute-done | bytes 1048608 | tf_op jit(solution)/shard_map/ppermute | solution.py:29
  162.0 3.7 %collective-permute-start.6 = (bf16[256,2048]{1,0:T(8,128)(2,1)}, bf16[256,2048]{1,0:T(8,128)(2,1)S(1)}, u32[]{:S(2)}, u32[]{:S(2)}) collective-permute-start(bf16[256,2048]{1,0:T(8,128)(2,1)} %collective-permute-done.5), channel_id=1, source_target_pairs={{1,0},{2,1},{3,2},{4,3},{5,4},{6,5},{7,6},{0,7},{9,8},{10,9},{11,1... | collective-permute-start | bytes 3145736 | tf_op jit(solution)/shard_map/ppermute | solution.py:31
  165.7 29.0 %collective-permute-done.3 = bf16[256,2048]{1,0:T(8,128)(2,1)} collective-permute-done((bf16[256,2048]{1,0:T(8,128)(2,1)}, bf16[256,2048]{1,0:T(8,128)(2,1)}, u32[]{:S(2)}, u32[]{:S(2)}) %collective-permute-start.3) | collective-permute-done | bytes 1048608 | tf_op jit(solution)/shard_map/ppermute | solution.py:29
  194.7 2.4 bitcast_dynamic-update-slice_fusion.7
  197.1 2.3 bitcast_dynamic-update-slice_fusion.6
  205.0 2.3 bitcast_dynamic-update-slice_fusion.1
  208.4 8.1 %gather_fusion = bf16[8,256,2048]{2,1,0:T(8,128)(2,1)} fusion(bf16[8,256,2048]{2,1,0:T(8,128)(2,1)} %bitcast_dynamic-update-slice_fusion, s32[1024]{0:T(1024)S(1)} %pad_clamp_fusion), kind=kCustom, calls=%fused_computation | custom fusion | bytes 16777248 | tf_op jit(solution)/shard_map/gather | solution.py:34
  216.4 10.5 %fusion.18 = f32[4,128,2048]{2,1,0:T(8,128)} fusion(bf16[4,128,2048]{2,1,0:T(8,128)(2,1)} %bitcast.59, bf16[2048,2048,1]{1,0,2:T(8,128)(2,1)} %bitcast.58), kind=kOutput, calls=%fused_computation.49 | convolution fusion | flops 4294967296 | bytes 14680064 | tf_op jit(solution)/shard_map/dot_general | solution.py:70
  227.0 5.1 %all-to-all-start = ((f32[4,128,2048]{2,1,0:T(8,128)}), f32[4,128,2048]{2,1,0:T(8,128)}, u32[]{:S(2)}, u32[]{:S(2)}) async-start(f32[4,128,2048]{2,1,0:T(8,128)} %fusion.18), calls=%async_computation | async-start | bytes 8388608 | tf_op jit(solution)/shard_map/all_to_all | solution.py:74
  234.4 2.9 copy.37
  237.3 2.9 copy.38
  240.2 35.3 %all-to-all-done = f32[4,128,2048]{2,1,0:T(8,128)} async-done(((f32[4,128,2048]{2,1,0:T(8,128)}), f32[4,128,2048]{2,1,0:T(8,128)}, u32[]{:S(2)}, u32[]{:S(2)}) %all-to-all-start) | async-done | bytes 4194336 | tf_op jit(solution)/shard_map/all_to_all | solution.py:74
  275.5 2.7 bitcast_reduce_fusion
  278.2 4.3 %gather_fusion.1 = bf16[256,2048]{1,0:T(8,128)(2,1)S(1)} fusion(bf16[2,128,2048]{2,1,0:T(8,128)(2,1)S(1)} %bitcast_reduce_fusion, s32[256]{0:T(256)S(1)} %reshape.177), kind=kCustom, calls=%fused_computation.1 | custom fusion | bytes 2099200 | tf_op jit(solution)/shard_map/gather | solution.py:76
  284.1 4.6 %reduce_sum.52 = bf16[128,2048]{1,0:T(8,128)(2,1)} reduce(bf16[128,2,2048]{2,1,0:T(2,128)(2,1)} %reshape.180, bf16[]{:T(256)} %constant.64.clone.1), dimensions={1}, to_apply=%region_6.7 | reduce | flops 262144 | bytes 1572866 | tf_op jit(solution)/shard_map/reduce_sum | solution.py:77
  288.7 6.3 %multiply_subtract_fusion = (f32[256,2048]{0,1:T(8,128)}, f32[256,2048]{0,1:T(8,128)}, f32[256,2048]{0,1:T(8,128)}) fusion(f32[256,2048]{0,1:T(8,128)S(1)} %copy-done.3, bf16[256,2048]{0,1:T(8,128)(2,1)} %reduce-scatter.2.cloned.1.call-done, f32[256,2048]{0,1:T(8,128)} %copy.37, f32[256,2048]{0,1:T(8,128)} %copy.38), kind=kLoop, calls=%fused_computation.12 | loop fusion | flops 8912896 | bytes 13631488 | tf_op jit(solution)/shard_map/sub | solution.py:42
  295.0 3.0 copy.41
  299.9 3.0 copy.43
  (61 shorter events, 22.7 us)
Async XLA Ops:
  7.2 16.9 %copy-start = (bf16[1,1,512,2048]{3,2,1,0:T(8,128)(2,1)S(1)}, bf16[1,1,512,2048]{3,2,1,0:T(8,128)(2,1)}, u32[]{:S(2)}) copy-start(bf16[1,1,512,2048]{3,2,1,0:T(8,128)(2,1)} %param.7) | copy-start | bytes 6291460
  7.2 281.5 %reduce-scatter.2.cloned.1.call-start = ((), (), s32[]{:S(2)}) async-start(), calls=%async_computation.2 | async-start | bytes 9437184 | tf_op jit(solution)/shard_map/reduce_scatter | solution.py:78
  22.8 1.3 copy-start.5
  30.9 1.6 copy-start.2
  32.7 31.0 %collective-permute-start = (bf16[256,2048]{1,0:T(8,128)(2,1)S(1)}, bf16[256,2048]{1,0:T(8,128)(2,1)S(1)}, u32[]{:S(2)}, u32[]{:S(2)}) collective-permute-start(bf16[256,2048]{1,0:T(8,128)(2,1)S(1)} %convert_element_type.25), channel_id=1, source_target_pairs={{0,1},{1,2},{2,3},{3,4},{4,5},{5,6},{6,7},{7,0},{8,9},{9,10},{10,1... | collective-permute-start | bytes 3145736 | tf_op jit(solution)/shard_map/ppermute | solution.py:29
  63.6 48.9 %collective-permute-start.1 = (bf16[256,2048]{1,0:T(8,128)(2,1)S(1)}, bf16[256,2048]{1,0:T(8,128)(2,1)S(1)}, u32[]{:S(2)}, u32[]{:S(2)}) collective-permute-start(bf16[256,2048]{1,0:T(8,128)(2,1)S(1)} %collective-permute-done), channel_id=1, source_target_pairs={{0,1},{1,2},{2,3},{3,4},{4,5},{5,6},{6,7},{7,0},{8,9},{9,10},{10,1... | collective-permute-start | bytes 3145736 | tf_op jit(solution)/shard_map/ppermute | solution.py:29
  63.7 49.1 %collective-permute-start.4 = (bf16[256,2048]{1,0:T(8,128)(2,1)S(1)}, bf16[256,2048]{1,0:T(8,128)(2,1)}, u32[]{:S(2)}, u32[]{:S(2)}) collective-permute-start(bf16[256,2048]{1,0:T(8,128)(2,1)S(1)} %convert_element_type.25), channel_id=1, source_target_pairs={{1,0},{2,1},{3,2},{4,3},{5,4},{6,5},{7,6},{0,7},{9,8},{10,9},{11,1... | collective-permute-start | bytes 3145736 | tf_op jit(solution)/shard_map/ppermute | solution.py:31
  112.5 1.0 copy-start.6
  112.5 49.2 %collective-permute-start.2 = (bf16[256,2048]{1,0:T(8,128)(2,1)S(1)}, bf16[256,2048]{1,0:T(8,128)(2,1)}, u32[]{:S(2)}, u32[]{:S(2)}) collective-permute-start(bf16[256,2048]{1,0:T(8,128)(2,1)S(1)} %collective-permute-done.1), channel_id=1, source_target_pairs={{0,1},{1,2},{2,3},{3,4},{4,5},{5,6},{6,7},{7,0},{8,9},{9,10},{10,1... | collective-permute-start | bytes 3145736 | tf_op jit(solution)/shard_map/ppermute | solution.py:29
  113.5 48.5 %collective-permute-start.5 = (bf16[256,2048]{1,0:T(8,128)(2,1)}, bf16[256,2048]{1,0:T(8,128)(2,1)}, u32[]{:S(2)}, u32[]{:S(2)}) collective-permute-start(bf16[256,2048]{1,0:T(8,128)(2,1)} %collective-permute-done.4), channel_id=1, source_target_pairs={{1,0},{2,1},{3,2},{4,3},{5,4},{6,5},{7,6},{0,7},{9,8},{10,9},{11,1... | collective-permute-start | bytes 3145736 | tf_op jit(solution)/shard_map/ppermute | solution.py:31
  161.7 33.0 %collective-permute-start.3 = (bf16[256,2048]{1,0:T(8,128)(2,1)}, bf16[256,2048]{1,0:T(8,128)(2,1)}, u32[]{:S(2)}, u32[]{:S(2)}) collective-permute-start(bf16[256,2048]{1,0:T(8,128)(2,1)} %collective-permute-done.2), channel_id=1, source_target_pairs={{0,1},{1,2},{2,3},{3,4},{4,5},{5,6},{6,7},{7,0},{8,9},{9,10},{10,1... | collective-permute-start | bytes 3145736 | tf_op jit(solution)/shard_map/ppermute | solution.py:29
  161.8 37.7 %copy-start.7 = (bf16[256,2048]{1,0:T(8,128)(2,1)S(1)}, bf16[256,2048]{1,0:T(8,128)(2,1)}, u32[]{:S(2)}) copy-start(bf16[256,2048]{1,0:T(8,128)(2,1)} %copy-done.6) | copy-start | bytes 3145732
  162.0 45.4 %collective-permute-start.6 = (bf16[256,2048]{1,0:T(8,128)(2,1)}, bf16[256,2048]{1,0:T(8,128)(2,1)S(1)}, u32[]{:S(2)}, u32[]{:S(2)}) collective-permute-start(bf16[256,2048]{1,0:T(8,128)(2,1)} %collective-permute-done.5), channel_id=1, source_target_pairs={{1,0},{2,1},{3,2},{4,3},{5,4},{6,5},{7,6},{0,7},{9,8},{10,9},{11,1... | collective-permute-start | bytes 3145736 | tf_op jit(solution)/shard_map/ppermute | solution.py:31
  227.0 48.5 %all-to-all-start = ((f32[4,128,2048]{2,1,0:T(8,128)}), f32[4,128,2048]{2,1,0:T(8,128)}, u32[]{:S(2)}, u32[]{:S(2)}) async-start(f32[4,128,2048]{2,1,0:T(8,128)} %fusion.18), calls=%async_computation | async-start | bytes 8388608 | tf_op jit(solution)/shard_map/all_to_all | solution.py:74
  232.1 2.0 copy-start.8
  282.5 6.2 %copy-start.3 = (f32[256,2048]{0,1:T(8,128)S(1)}, f32[256,2048]{0,1:T(8,128)}, u32[]{:S(2)}) copy-start(f32[256,2048]{0,1:T(8,128)} %copy.40) | copy-start | bytes 6291460
  295.0 3.0 copy-start.4
  299.9 3.0 copy-start.1
Sparse Core Ops, SparseCore 0:
  31.1 147.8 reduce-scatter.1
